TPU v7x, 128 devices: a whole 4x4x4 slice. The times are simulated.
128 devices in a mesh: space: 32 (over y, x, core), shell: 4 (over z).
Axes of the slice: x: 4, y: 4, z: 4, core: 2. Of those that a mesh axis runs over, the one named last changes fastest.
Arguments:
- weights: float32 [262144], P(('space', 'shell')), may hold values from 0.02 to 1.5
- seg_streamline: int32 [32, 4, 32, 256], P('space', 'shell'), may hold values from 0 to 2047
- seg_features: float32 [32, 4, 32, 256, 128], P('space', 'shell'), may hold values from -12 to 12
- pair_counts: int32 [32, 4, 32], P('space', 'shell'), may hold values from 32 to 256, as said below
- seg_voxel: int32 [32, 4, 32, 256], P('space', 'shell'), may hold values from 0 to 4095
- dictionary: float32 [128, 256], P(None, 'shell'), may hold values from -0.375 to 0.375
- measured: float32 [256, 131072], P('shell', 'space'), may hold values from -6 to 6
Outputs:
- new_weights: float32 [262144], P(('space', 'shell'))
- residual: float32 [256, 131072], P('shell', 'space')
Inputs may be any that keep to these rules, and one draw needn't show every extreme that they name: In each shell group q one voxel block d has pair_counts[s, q, d] = 256 for every s.
All inputs are finite; a program needn't handle non-finite values.
Results may differ from a plain program's by a relative error of at most 0.0003.
Values sent between devices are 32-bit elements; how exact they have to be, the bound alone decides.
No kernel may reach another device: no remote copies, remote signals or barrier semaphores. Data moves between devices by JAX's collectives and lax.ppermute only.
A program may use at most 64 MiB of HBM per device.

v0:
```python
import jax
import jax.numpy as jnp
from jax import lax
from jax.sharding import PartitionSpec as P

ITERS = 2
HI = lax.Precision.HIGHEST


def one_hot_pair(index, count):
    low_count = 64
    high_count = count // low_count
    flat = index.reshape(-1)
    high = (flat // low_count)[:, None] == lax.broadcasted_iota(jnp.int32, (1, high_count), 1)
    low = (flat % low_count)[:, None] == lax.broadcasted_iota(jnp.int32, (1, low_count), 1)
    return (high.astype(jnp.float32), low.astype(jnp.float32))


def pick(table, high, low):
    rows = jnp.dot(high, table.reshape(high.shape[1], low.shape[1]), precision=HI)
    return jnp.sum(rows * low, axis=1)


def spread(values, high, low):
    return jnp.dot(high.T, values.reshape(-1)[:, None] * low, precision=HI).reshape(-1)


def on_device(weights, seg_streamline, seg_features, pair_counts, seg_voxel, dictionary, measured):
    blocks = seg_streamline.shape[2]
    slots = seg_streamline.shape[3]
    coeffs = seg_features.shape[4]
    streams = weights.shape[0]
    stream_index = seg_streamline.reshape(blocks, slots)
    voxel_index = seg_voxel.reshape(blocks * slots)
    counts = pair_counts.reshape(blocks)
    live_slot = lax.broadcasted_iota(jnp.int32, (blocks, slots), 1) < counts[:, None]
    masked = jnp.where(
        live_slot[:, :, None], seg_features.reshape(blocks, slots, coeffs), jnp.float32(0.0)
    )
    half = slots // 2
    feat_parts = [
        lax.all_to_all(masked[:, h * half : (h + 1) * half], "space", 0, 0, tiled=True)
        for h in range(2)
    ]
    gram = lax.psum(jnp.dot(dictionary, dictionary.T, precision=HI), "shell")
    data_proj = lax.psum(jnp.dot(measured.T, dictionary.T, precision=HI), "shell")
    feat_parts[1], gram, data_proj = lax.optimization_barrier((feat_parts[1], gram, data_proj))
    vox_parts = [
        voxel_index.reshape(blocks, slots)[:, h * half : (h + 1) * half].reshape(-1)
        for h in range(2)
    ]
    local_feat = jnp.concatenate(feat_parts, axis=1).reshape(blocks * slots, coeffs)
    high, low = one_hot_pair(stream_index, streams)
    column_sq = spread(jnp.sum(masked * masked, axis=2), high, low)
    scaling = 0.5 / (0.5 + column_sq)
    current = weights
    residual = jnp.zeros(measured.shape, jnp.float32)
    for iteration in range(ITERS):
        picked = pick(current, high, low).reshape(blocks, slots)
        local_x = lax.all_to_all(picked, "space", split_axis=0, concat_axis=0, tiled=True)
        partial_coeff = jnp.zeros((measured.shape[1], coeffs), jnp.float32)
        for h in range(2):
            part_x = local_x[:, h * half : (h + 1) * half].reshape(-1, 1)
            partial_coeff = partial_coeff.at[vox_parts[h]].add(
                part_x * feat_parts[h].reshape(-1, coeffs)
            )
        coeff_sum = lax.psum(partial_coeff, "shell")
        if iteration == ITERS - 1:
            residual = jnp.einsum("jg,vj->gv", dictionary, coeff_sum, precision=HI) - measured
        adjoint = jnp.dot(coeff_sum, gram, precision=HI) - data_proj
        local_grad = jnp.sum(local_feat * adjoint[voxel_index], axis=1).reshape(blocks, slots)
        grad_slot = lax.all_to_all(local_grad, "space", split_axis=0, concat_axis=0, tiled=True)
        gradient = spread(grad_slot, high, low)
        current = jnp.maximum(current - scaling * gradient, 0.0)
    return (current, residual)


def solution(mesh):
    in_specs = (
        P(("space", "shell")),
        P("space", "shell", None, None),
        P("space", "shell", None, None, None),
        P("space", "shell", None),
        P("space", "shell", None, None),
        P(None, "shell"),
        P("shell", "space"),
    )
    out_specs = (P(("space", "shell")), P("shell", "space"))
    return jax.shard_map(
        on_device, mesh=mesh, in_specs=in_specs, out_specs=out_specs, check_vma=False
    )
```

profile of v0, /device:TPU:1, one launch (start us, length us, event | category | flops | bytes accessed | tf_op | source)
XLA Modules:
  0.0 421.6 jit_solution(4449629302932283)
XLA Ops:
  8.8 1.8 fusion.9
  10.6 8.6 %all-to-all-start.2 = ((f32[32,1,256]{2,1,0:T(1,128)}), f32[32,1,256]{2,1,0:T(1,128)S(1)}, u32[]{:S(2)}, u32[]{:S(2)}) async-start(f32[32,1,256]{2,1,0:T(1,128)} %bitcast.6), calls=%async_computation.2 | async-start | bytes 65536 | tf_op jit(solution)/shard_map/all_to_all | solution.py:60
  19.3 4.5 %multiply_reduce_fusion = (f32[32,256]{1,0:T(8,128)S(1)}, f32[32,256,128]{2,1,0:T(8,128)S(1)}) fusion(f32[1,1,32,256,128]{4,3,2,1,0:T(8,128)} %param.9, pred[32,256]{1,0:T(8,128)(4,1)S(1)} %iota_compare_fusion.10), kind=kLoop, calls=%fused_computation.18 | loop fusion | flops 3137536 | bytes 8429568 | tf_op jit(solution)/shard_map/reduce_sum | solution.py:54
  23.8 2.2 fusion.46
  26.5 7.1 %all-to-all-start = ((f32[32,128,128]{2,1,0:T(8,128)}), f32[32,128,128]{2,1,0:T(8,128)S(1)}, u32[]{:S(2)}, u32[]{:S(2)}) async-start(f32[32,128,128]{2,1,0:T(8,128)} %get-tuple-element.12), calls=%async_computation | async-start | bytes 4194304 | tf_op jit(solution)/shard_map/all_to_all | solution.py:42
  34.5 4.8 %fusion.49 = f32[4096,128]{1,0:T(8,128)} fusion(f32[64,4096]{1,0:T(8,128)S(1)} %copy-done.6, f32[128,64]{0,1:T(8,128)S(1)} %copy-done), kind=kOutput, calls=%fused_computation.82 | convolution fusion | flops 402653184 | bytes 3178496 | tf_op jit(solution)/shard_map/dot_general | solution.py:46
  39.4 21.9 %all-to-all-done = f32[32,128,128]{2,1,0:T(8,128)S(1)} async-done(((f32[32,128,128]{2,1,0:T(8,128)}), f32[32,128,128]{2,1,0:T(8,128)S(1)}, u32[]{:S(2)}, u32[]{:S(2)}) %all-to-all-start) | async-done | bytes 2097184 | tf_op jit(solution)/shard_map/all_to_all | solution.py:42
  61.4 6.7 %all-to-all-start.1 = ((f32[32,128,128]{2,1,0:T(8,128)}), f32[32,128,128]{2,1,0:T(8,128)}, u32[]{:S(2)}, u32[]{:S(2)}) async-start(f32[32,128,128]{2,1,0:T(8,128)} %get-tuple-element.13), calls=%async_computation.1 | async-start | bytes 4194304 | tf_op jit(solution)/shard_map/all_to_all | solution.py:42
  68.2 1.9 bitcast_multiply_fusion.5
  70.2 23.2 %scatter_custom_fusion = f32[4096,128]{1,0:T(8,128)S(1)} fusion(s32[4096]{0:T(1024)S(1)} %bitcast.83, f32[4096,128]{1,0:T(8,128)} %bitcast_multiply_fusion.5, f32[]{:T(128)} %constant.42.clone.1), kind=kCustom, calls=%fused_computation.40 | custom fusion | flops 524288 | bytes 2097664 | tf_op jit(solution)/shard_map/scatter-add | solution.py:64
  93.3 2.8 all-to-all-done.1
  96.1 5.6 %all-reduce.9.cloned.1.call-done = (f32[128,128]{1,0:T(8,128)}, f32[4096,128]{1,0:T(8,128)}) async-done(((f32[128,128]{1,0:T(8,128)}, f32[4096,128]{1,0:T(8,128)}), (f32[128,128]{1,0:T(8,128)}, f32[4096,128]{1,0:T(8,128)})) %all-reduce.9.cloned.1.call-update) | async-done | bytes 2162704 | tf_op jit(solution)/shard_map/psum | solution.py:45
  101.7 3.5 bitcast_multiply_fusion.3
  105.3 23.6 %scatter_fusion = f32[4096,128]{1,0:T(8,128)S(1)} fusion(f32[4096,128]{1,0:T(8,128)S(1)} %scatter_custom_fusion, s32[4096]{0:T(1024)S(1)} %bitcast.67, f32[4096,128]{1,0:T(8,128)} %bitcast_multiply_fusion.3), kind=kCustom, calls=%fused_computation.3 | custom fusion | flops 524288 | bytes 6307840 | tf_op jit(solution)/shard_map/scatter-add | solution.py:64
  130.3 4.7 %pad_maximum_fusion = f32[32,256,128]{2,1,0:T(8,128)} fusion(f32[32,128,128]{2,1,0:T(8,128)} %all-to-all-done.1, f32[32,128,128]{2,1,0:T(8,128)} %copy-done.3), kind=kLoop, calls=%fused_computation.12 | loop fusion | flops 1048576 | bytes 8388608 | tf_op jit(solution)/shard_map/concatenate | solution.py:52
  135.0 54.1 %all-reduce.5.cloned.1.call-done = f32[4096,128]{1,0:T(8,128)} async-done(((f32[4096,128]{1,0:T(8,128)}), f32[4096,128]{1,0:T(8,128)}) %all-reduce.5.cloned.1.call-update) | async-done | bytes 2097168 | tf_op jit(solution)/shard_map/psum | solution.py:67
  189.0 4.0 convolution_subtract_fusion.1
  193.0 27.7 %gather_fusion = f32[8192,128]{1,0:T(8,128)} fusion(f32[4096,128]{1,0:T(8,128)S(1)} %convolution_subtract_fusion.1, s32[8192]{0:T(1024)S(1)} %broadcast_clamp_fusion), kind=kCustom, calls=%fused_computation | custom fusion | bytes 8421376 | tf_op jit(solution)/shard_map/gather | solution.py:71
  220.7 5.2 %fusion.1 = f32[8192]{0:T(1024)} fusion(f32[8192,128]{1,0:T(8,128)} %gather_fusion, f32[32,256,128]{2,1,0:T(8,128)} %pad_maximum_fusion), kind=kLoop, calls=%fused_computation.15 | loop fusion | flops 2088960 | bytes 8421376 | tf_op jit(solution)/shard_map/reduce_sum | solution.py:71
  226.0 7.7 %all-to-all-start.3 = ((f32[32,1,256]{2,1,0:T(1,128)}), f32[32,1,256]{2,1,0:T(1,128)S(1)}, u32[]{:S(2)}, u32[]{:S(2)}) async-start(f32[32,1,256]{2,1,0:T(1,128)} %bitcast.14), calls=%async_computation.3 | async-start | bytes 65536 | tf_op jit(solution)/shard_map/all_to_all | solution.py:72
  235.1 5.8 %all-to-all-done.3 = f32[32,1,256]{2,1,0:T(1,128)S(1)} async-done(((f32[32,1,256]{2,1,0:T(1,128)}), f32[32,1,256]{2,1,0:T(1,128)S(1)}, u32[]{:S(2)}, u32[]{:S(2)}) %all-to-all-start.3) | async-done | bytes 32800 | tf_op jit(solution)/shard_map/all_to_all | solution.py:72
  243.7 10.7 %all_to_all.52 = f32[32,1,256]{2,1,0:T(1,128)S(1)} all-to-all(f32[32,1,256]{2,1,0:T(1,128)S(1)} %bitcast.82), channel_id=1, replica_groups=mesh['space'=32,'shell'=4] {'space'}, dimensions={0} | all-to-all | bytes 65536 | tf_op jit(solution)/shard_map/all_to_all | solution.py:60
  254.5 3.8 bitcast_multiply_fusion.2
  258.3 23.2 %scatter_custom_fusion.2 = f32[4096,128]{1,0:T(8,128)S(1)} fusion(s32[4096]{0:T(1024)S(1)} %bitcast.84, f32[4096,128]{1,0:T(8,128)} %get-tuple-element.23, f32[]{:T(128)} %constant.42.clone.1), kind=kCustom, calls=%fused_computation.38 | custom fusion | flops 524288 | bytes 2097664 | tf_op jit(solution)/shard_map/scatter-add | solution.py:64
  281.4 23.4 %scatter_fusion.1 = f32[4096,128]{1,0:T(8,128)S(1)} fusion(f32[4096,128]{1,0:T(8,128)S(1)} %scatter_custom_fusion.2, s32[4096]{0:T(1024)S(1)} %bitcast.68, f32[4096,128]{1,0:T(8,128)} %get-tuple-element.22), kind=kCustom, calls=%fused_computation.5 | custom fusion | flops 524288 | bytes 6307840 | tf_op jit(solution)/shard_map/scatter-add | solution.py:64
  306.2 54.9 %all-reduce.7.cloned.1.call-done = f32[4096,128]{1,0:T(8,128)} async-done(((f32[4096,128]{1,0:T(8,128)}), f32[4096,128]{1,0:T(8,128)}) %all-reduce.7.cloned.1.call-update) | async-done | bytes 2097168 | tf_op jit(solution)/shard_map/psum | solution.py:67
  361.2 4.0 convolution_subtract_fusion
  365.2 27.7 %gather_fusion.1 = f32[8192,128]{1,0:T(8,128)} fusion(f32[4096,128]{1,0:T(8,128)S(1)} %convolution_subtract_fusion, s32[8192]{0:T(1024)S(1)} %broadcast_clamp_fusion), kind=kCustom, calls=%fused_computation.1 | custom fusion | bytes 8421376 | tf_op jit(solution)/shard_map/gather | solution.py:71
  392.9 5.4 %fusion.2 = f32[8192]{0:T(1024)} fusion(f32[8192,128]{1,0:T(8,128)} %gather_fusion.1, f32[32,256,128]{2,1,0:T(8,128)} %pad_maximum_fusion), kind=kLoop, calls=%fused_computation.16 | loop fusion | flops 2088960 | bytes 8421376 | tf_op jit(solution)/shard_map/reduce_sum | solution.py:71
  398.2 7.5 %all-to-all-start.5 = ((f32[32,1,256]{2,1,0:T(1,128)}), f32[32,1,256]{2,1,0:T(1,128)S(1)}, u32[]{:S(2)}, u32[]{:S(2)}) async-start(f32[32,1,256]{2,1,0:T(1,128)} %bitcast.19), calls=%async_computation.5 | async-start | bytes 65536 | tf_op jit(solution)/shard_map/all_to_all | solution.py:72
  405.8 3.4 fusion
  409.1 3.9 all-to-all-done.5
  (54 shorter events, 12.4 us)
Async XLA Ops:
  7.2 26.4 %copy-start = (f32[128,64]{0,1:T(8,128)S(1)}, f32[128,64]{0,1:T(8,128)}, u32[]{:S(2)}) copy-start(f32[128,64]{0,1:T(8,128)} %param.12) | copy-start | bytes 98308
  7.2 12.0 %copy-start.10 = (s32[1,1,32]{2,1,0:T(1,128)S(1)}, s32[1,1,32]{2,1,0:T(1,128)}, u32[]{:S(2)}) copy-start(s32[1,1,32]{2,1,0:T(1,128)} %param.10) | copy-start | bytes 388
  10.6 15.8 %all-to-all-start.2 = ((f32[32,1,256]{2,1,0:T(1,128)}), f32[32,1,256]{2,1,0:T(1,128)S(1)}, u32[]{:S(2)}, u32[]{:S(2)}) async-start(f32[32,1,256]{2,1,0:T(1,128)} %bitcast.6), calls=%async_computation.2 | async-start | bytes 65536 | tf_op jit(solution)/shard_map/all_to_all | solution.py:60
  26.5 8.1 %copy-start.6 = (f32[64,4096]{1,0:T(8,128)S(1)}, f32[64,4096]{1,0:T(8,128)}, u32[]{:S(2)}) copy-start(f32[64,4096]{1,0:T(8,128)} %param.13) | copy-start | bytes 3145732
  26.5 34.9 %all-to-all-start = ((f32[32,128,128]{2,1,0:T(8,128)}), f32[32,128,128]{2,1,0:T(8,128)S(1)}, u32[]{:S(2)}, u32[]{:S(2)}) async-start(f32[32,128,128]{2,1,0:T(8,128)} %get-tuple-element.12), calls=%async_computation | async-start | bytes 4194304 | tf_op jit(solution)/shard_map/all_to_all | solution.py:42
  33.6 68.2 %all-reduce.9.cloned.1.call-start = ((), (), s32[]{:S(2)}) async-start(), calls=%async_computation.8 | async-start | bytes 4325376 | tf_op jit(solution)/shard_map/psum | solution.py:45
  34.5 4.8 %copy-start.8 = (s32[1,1,32,256]{3,2,1,0:T(8,128)S(1)}, s32[1,1,32,256]{3,2,1,0:T(8,128)}, u32[]{:S(2)}) copy-start(s32[1,1,32,256]{3,2,1,0:T(8,128)} %param.11) | copy-start | bytes 98308
  61.4 6.8 %copy-start.3 = (f32[32,128,128]{2,1,0:T(8,128)}, f32[32,128,128]{2,1,0:T(8,128)S(1)}, u32[]{:S(2)}) copy-start(f32[32,128,128]{2,1,0:T(8,128)S(1)} %all-to-all-done) | copy-start | bytes 6291460
  61.4 34.7 %all-to-all-start.1 = ((f32[32,128,128]{2,1,0:T(8,128)}), f32[32,128,128]{2,1,0:T(8,128)}, u32[]{:S(2)}, u32[]{:S(2)}) async-start(f32[32,128,128]{2,1,0:T(8,128)} %get-tuple-element.13), calls=%async_computation.1 | async-start | bytes 4194304 | tf_op jit(solution)/shard_map/all_to_all | solution.py:42
  68.1 120.9 %all-reduce.5.cloned.1.call-start = ((), (), s32[]{:S(2)}) async-start(), calls=%async_computation.6 | async-start | bytes 4194304 | tf_op jit(solution)/shard_map/psum | solution.py:67
  128.9 1.3 copy-start.1
  130.3 58.7 %copy-start.7 = (f32[128,128]{1,0:T(8,128)S(1)}, f32[128,128]{1,0:T(8,128)}, u32[]{:S(2)}) copy-start(f32[128,128]{1,0:T(8,128)} %get-tuple-element.6) | copy-start | bytes 196612
  226.0 16.4 %copy-start.9 = (f32[2048]{0:T(1024)S(1)}, f32[2048]{0:T(1024)}, u32[]{:S(2)}) copy-start(f32[2048]{0:T(1024)} %param.7) | copy-start | bytes 24580
  226.0 14.9 %all-to-all-start.3 = ((f32[32,1,256]{2,1,0:T(1,128)}), f32[32,1,256]{2,1,0:T(1,128)S(1)}, u32[]{:S(2)}, u32[]{:S(2)}) async-start(f32[32,1,256]{2,1,0:T(1,128)} %bitcast.14), calls=%async_computation.3 | async-start | bytes 65536 | tf_op jit(solution)/shard_map/all_to_all | solution.py:72
  233.6 127.5 %all-reduce.7.cloned.1.call-start = ((), (), s32[]{:S(2)}) async-start(), calls=%async_computation.7 | async-start | bytes 4194304 | tf_op jit(solution)/shard_map/psum | solution.py:67
  240.9 13.6 %copy-start.4 = (f32[32,128,128]{2,1,0:T(8,128)S(1)}, f32[32,128,128]{2,1,0:T(8,128)}, u32[]{:S(2)}) copy-start(f32[32,128,128]{2,1,0:T(8,128)} %copy-done.3) | copy-start | bytes 6291460
  304.9 1.3 copy-start.2
  392.9 12.9 %copy-start.5 = (f32[4096,128]{1,0:T(8,128)S(1)}, f32[4096,128]{1,0:T(8,128)}, u32[]{:S(2)}) copy-start(f32[4096,128]{1,0:T(8,128)} %all-reduce.7.cloned.1.call-done) | copy-start | bytes 6291460
  398.2 14.8 %all-to-all-start.5 = ((f32[32,1,256]{2,1,0:T(1,128)}), f32[32,1,256]{2,1,0:T(1,128)S(1)}, u32[]{:S(2)}, u32[]{:S(2)}) async-start(f32[32,1,256]{2,1,0:T(1,128)} %bitcast.19), calls=%async_computation.5 | async-start | bytes 65536 | tf_op jit(solution)/shard_map/all_to_all | solution.py:72
Sparse Core Ops, SparseCore 0:
  39.4 62.2 all-reduce.8
  130.4 58.6 all-reduce.4
  306.3 54.7 all-reduce.6
where the time goes:
time: 422 us
  waiting for transfers between devices  149 us (35%)
  other arithmetic  123 us (29%)
  local copies, waits for them, and re-layouts  62.1 us (15%)
  starting transfers between devices  37.7 us (9%)
  matrix products  24.4 us (6%)
  between operations  14 us (3%)
  blocking collectives  10.7 us (3%)
    psum x2, waiting for transfers between devices, on_device(): coeff_sum = lax.psum(partial_coeff, 'shell')  109 us
    scatter-add x4, other arithmetic, on_device(): partial_coeff.at[vox_parts[h]]  93.4 us
    gather x2, local copies, waits for them, and re-layouts, on_device(): adjoint[voxel_index]  55.4 us
    all_to_all x2, waiting for transfers between devices, on_device(): lax.all_to_all(masked[:, h * half:(h + 1) * half], 'space', 0, 0, tiled=T...  24.7 us
    all_to_all x2, starting transfers between devices, on_device(): lax.all_to_all(local_grad, 'space', split_axis=0, concat_axis=0, tiled=True)  15.2 us
    all_to_all x2, starting transfers between devices, on_device(): lax.all_to_all(masked[:, h * half:(h + 1) * half], 'space', 0, 0, tiled=T...  13.8 us
    all_to_all x1, blocking collectives, on_device(): lax.all_to_all(picked, 'space', split_axis=0, concat_axis=0, tiled=True)  10.7 us
    reduce_sum x2, other arithmetic, on_device(): jnp.sum(local_feat * adjoint[voxel_index], axis=1).reshape(blocks, slots)  10.6 us
  transfers between devices with their start and end apart: 8, of which 8 were waited for; matrix products, arithmetic and copies ran while one was open for 11% of the time, Pallas kernels for 0%

commit v1 on v0

--- a/solution.py
+++ b/solution.py
@@ -64,7 +64,8 @@
             partial_coeff = partial_coeff.at[vox_parts[h]].add(
                 part_x * feat_parts[h].reshape(-1, coeffs)
             )
-        coeff_sum = lax.psum(partial_coeff, "shell")
+        current_value = lax.all_gather(partial_coeff, "shell")
+        coeff_sum = jnp.sum(current_value, axis=0)
         if iteration == ITERS - 1:
             residual = jnp.einsum("jg,vj->gv", dictionary, coeff_sum, precision=HI) - measured
         adjoint = jnp.dot(coeff_sum, gram, precision=HI) - data_proj

time: 422 us -> 483 us (1.14)
  waiting for transfers between devices: 149 us -> 199 us
  other arithmetic: 123 us -> 134 us
    all_gather x0 -> x2, waiting for transfers between devices: none -> 159 us  [on_device(): current_value = lax.all_gather(partial_coeff, 'shell')]
    psum x2 -> x0, waiting for transfers between devices: 109 us -> none  [on_device(): coeff_sum = lax.psum(partial_coeff, 'shell')]
    reduce_sum x0 -> x2, other arithmetic: none -> 10.7 us  [on_device(): coeff_sum = jnp.sum(current_value, axis=0)]
  transfers between devices with their start and end apart: 8 -> 8, of which waited for: 8 -> 8; matrix products, arithmetic and copies ran while one was open for 11% -> 10% of each run, Pallas kernels for 0% -> 0%
where the time goes in v1:
time: 483 us; the launch traced here: 482 us
  waiting for transfers between devices  199 us (41%)
  other arithmetic  134 us (28%)
  local copies, waits for them, and re-layouts  62.2 us (13%)
  starting transfers between devices  37.8 us (8%)
  matrix products  24.4 us (5%)
  between operations  14 us (3%)
  blocking collectives  10.7 us (2%)
    all_gather x2, waiting for transfers between devices, on_device(): current_value = lax.all_gather(partial_coeff, 'shell')  159 us
    scatter-add x4, other arithmetic, on_device(): partial_coeff.at[vox_parts[h]]  93.4 us
    gather x2, local copies, waits for them, and re-layouts, on_device(): adjoint[voxel_index]  55.5 us
    all_to_all x2, waiting for transfers between devices, on_device(): lax.all_to_all(masked[:, h * half:(h + 1) * half], 'space', 0, 0, tiled=T...  24.8 us
    all_to_all x2, starting transfers between devices, on_device(): lax.all_to_all(local_grad, 'space', split_axis=0, concat_axis=0, tiled=True)  15.3 us
    all_to_all x2, starting transfers between devices, on_device(): lax.all_to_all(masked[:, h * half:(h + 1) * half], 'space', 0, 0, tiled=T...  13.8 us
    all_to_all x1, blocking collectives, on_device(): lax.all_to_all(picked, 'space', split_axis=0, concat_axis=0, tiled=True)  10.7 us
    reduce_sum x2, other arithmetic, on_device(): coeff_sum = jnp.sum(current_value, axis=0)  10.7 us
  transfers between devices with their start and end apart: 8, of which 8 were waited for; matrix products, arithmetic and copies ran while one was open for 10% of the time, Pallas kernels for 0%

profile of v1, /device:TPU:1, one launch (start us, length us, event | category | flops | bytes accessed | tf_op | source)
XLA Modules:
  0.0 482.3 jit_solution(16653392294861999275)
XLA Ops:
  10.6 8.6 %all-to-all-start.2 = ((f32[32,1,256]{2,1,0:T(1,128)}), f32[32,1,256]{2,1,0:T(1,128)S(1)}, u32[]{:S(2)}, u32[]{:S(2)}) async-start(f32[32,1,256]{2,1,0:T(1,128)} %bitcast.6), calls=%async_computation.2 | async-start | bytes 65536 | tf_op jit(solution)/shard_map/all_to_all | solution.py:60
  19.3 4.5 multiply_reduce_fusion
  23.8 2.2 fusion.46
  26.5 7.1 %all-to-all-start = ((f32[32,128,128]{2,1,0:T(8,128)}), f32[32,128,128]{2,1,0:T(8,128)S(1)}, u32[]{:S(2)}, u32[]{:S(2)}) async-start(f32[32,128,128]{2,1,0:T(8,128)} %get-tuple-element.12), calls=%async_computation | async-start | bytes 4194304 | tf_op jit(solution)/shard_map/all_to_all | solution.py:42
  34.5 4.8 fusion.49
  39.4 22.0 %all-to-all-done = f32[32,128,128]{2,1,0:T(8,128)S(1)} async-done(((f32[32,128,128]{2,1,0:T(8,128)}), f32[32,128,128]{2,1,0:T(8,128)S(1)}, u32[]{:S(2)}, u32[]{:S(2)}) %all-to-all-start) | async-done | bytes 2097184 | tf_op jit(solution)/shard_map/all_to_all | solution.py:42
  61.4 6.7 %all-to-all-start.1 = ((f32[32,128,128]{2,1,0:T(8,128)}), f32[32,128,128]{2,1,0:T(8,128)}, u32[]{:S(2)}, u32[]{:S(2)}) async-start(f32[32,128,128]{2,1,0:T(8,128)} %get-tuple-element.13), calls=%async_computation.1 | async-start | bytes 4194304 | tf_op jit(solution)/shard_map/all_to_all | solution.py:42
  70.2 23.2 %scatter_custom_fusion = f32[4096,128]{1,0:T(8,128)S(1)} fusion(s32[4096]{0:T(1024)S(1)} %bitcast.87, f32[4096,128]{1,0:T(8,128)} %bitcast_multiply_fusion.5, f32[]{:T(128)} %constant.42.clone.1), kind=kCustom, calls=%fused_computation.40 | custom fusion | flops 524288 | bytes 2097664 | tf_op jit(solution)/shard_map/scatter-add | solution.py:64
  93.3 2.8 all-to-all-done.1
  96.1 5.6 %all-reduce.3.cloned.1.call-done = (f32[128,128]{1,0:T(8,128)}, f32[4096,128]{1,0:T(8,128)}) async-done(((f32[128,128]{1,0:T(8,128)}, f32[4096,128]{1,0:T(8,128)}), (f32[128,128]{1,0:T(8,128)}, f32[4096,128]{1,0:T(8,128)})) %all-reduce.3.cloned.1.call-update) | async-done | bytes 2162704 | tf_op jit(solution)/shard_map/psum | solution.py:45
  101.7 3.5 bitcast_multiply_fusion.3
  105.3 23.6 %scatter_fusion = f32[4096,128]{1,0:T(8,128)S(1)} fusion(f32[4096,128]{1,0:T(8,128)S(1)} %scatter_custom_fusion, s32[4096]{0:T(1024)S(1)} %bitcast.71, f32[4096,128]{1,0:T(8,128)} %bitcast_multiply_fusion.3), kind=kCustom, calls=%fused_computation.3 | custom fusion | flops 524288 | bytes 6307840 | tf_op jit(solution)/shard_map/scatter-add | solution.py:64
  130.3 4.6 pad_maximum_fusion
  135.0 78.3 %all-gather.5.cloned.1.call-done = f32[16384,128]{1,0:T(8,128)} async-done(((f32[4096,128]{1,0:T(8,128)}), f32[16384,128]{1,0:T(8,128)}) %all-gather.5.cloned.1.call-update) | async-done | bytes 8388624 | tf_op jit(solution)/shard_map/all_gather | solution.py:67
  213.3 5.4 %reduce_sum.65 = f32[4096,128]{1,0:T(8,128)} reduce(f32[4,4096,128]{2,1,0:T(8,128)} %bitcast.69, f32[]{:T(128)} %constant.42.clone.1), dimensions={0}, to_apply=%region_6.7 | reduce | flops 1572864 | bytes 10485764 | tf_op jit(solution)/shard_map/reduce_sum | solution.py:68
  218.7 4.0 convolution_subtract_fusion.1
  222.7 27.8 %gather_fusion = f32[8192,128]{1,0:T(8,128)} fusion(f32[4096,128]{1,0:T(8,128)S(1)} %convolution_subtract_fusion.1, s32[8192]{0:T(1024)S(1)} %broadcast_clamp_fusion), kind=kCustom, calls=%fused_computation | custom fusion | bytes 8421376 | tf_op jit(solution)/shard_map/gather | solution.py:72
  250.5 5.2 %fusion.1 = f32[8192]{0:T(1024)} fusion(f32[8192,128]{1,0:T(8,128)} %gather_fusion, f32[32,256,128]{2,1,0:T(8,128)} %pad_maximum_fusion), kind=kLoop, calls=%fused_computation.15 | loop fusion | flops 2088960 | bytes 8421376 | tf_op jit(solution)/shard_map/reduce_sum | solution.py:72
  255.7 7.7 %all-to-all-start.3 = ((f32[32,1,256]{2,1,0:T(1,128)}), f32[32,1,256]{2,1,0:T(1,128)S(1)}, u32[]{:S(2)}, u32[]{:S(2)}) async-start(f32[32,1,256]{2,1,0:T(1,128)} %bitcast.15), calls=%async_computation.3 | async-start | bytes 65536 | tf_op jit(solution)/shard_map/all_to_all | solution.py:73
  264.9 5.8 %all-to-all-done.3 = f32[32,1,256]{2,1,0:T(1,128)S(1)} async-done(((f32[32,1,256]{2,1,0:T(1,128)}), f32[32,1,256]{2,1,0:T(1,128)S(1)}, u32[]{:S(2)}, u32[]{:S(2)}) %all-to-all-start.3) | async-done | bytes 32800 | tf_op jit(solution)/shard_map/all_to_all | solution.py:73
  273.5 10.7 %all_to_all.52 = f32[32,1,256]{2,1,0:T(1,128)S(1)} all-to-all(f32[32,1,256]{2,1,0:T(1,128)S(1)} %bitcast.86), channel_id=1, replica_groups=mesh['space'=32,'shell'=4] {'space'}, dimensions={0} | all-to-all | bytes 65536 | tf_op jit(solution)/shard_map/all_to_all | solution.py:60
  284.2 3.8 bitcast_multiply_fusion.2
  288.0 23.2 %scatter_custom_fusion.2 = f32[4096,128]{1,0:T(8,128)S(1)} fusion(s32[4096]{0:T(1024)S(1)} %bitcast.88, f32[4096,128]{1,0:T(8,128)} %get-tuple-element.23, f32[]{:T(128)} %constant.42.clone.1), kind=kCustom, calls=%fused_computation.38 | custom fusion | flops 524288 | bytes 2097664 | tf_op jit(solution)/shard_map/scatter-add | solution.py:64
  311.2 23.4 %scatter_fusion.1 = f32[4096,128]{1,0:T(8,128)S(1)} fusion(f32[4096,128]{1,0:T(8,128)S(1)} %scatter_custom_fusion.2, s32[4096]{0:T(1024)S(1)} %bitcast.72, f32[4096,128]{1,0:T(8,128)} %get-tuple-element.22), kind=kCustom, calls=%fused_computation.5 | custom fusion | flops 524288 | bytes 6307840 | tf_op jit(solution)/shard_map/scatter-add | solution.py:64
  335.9 80.4 %all-gather.7.cloned.1.call-done = f32[16384,128]{1,0:T(8,128)} async-done(((f32[4096,128]{1,0:T(8,128)}), f32[16384,128]{1,0:T(8,128)}) %all-gather.7.cloned.1.call-update) | async-done | bytes 8388624 | tf_op jit(solution)/shard_map/all_gather | solution.py:67
  416.4 5.4 %reduce_sum.68 = f32[4096,128]{1,0:T(8,128)} reduce(f32[4,4096,128]{2,1,0:T(8,128)} %bitcast.70, f32[]{:T(128)} %constant.42.clone.1), dimensions={0}, to_apply=%region_11.12 | reduce | flops 1572864 | bytes 10485764 | tf_op jit(solution)/shard_map/reduce_sum | solution.py:68
  421.7 4.0 convolution_subtract_fusion
  425.8 27.8 %gather_fusion.1 = f32[8192,128]{1,0:T(8,128)} fusion(f32[4096,128]{1,0:T(8,128)S(1)} %convolution_subtract_fusion, s32[8192]{0:T(1024)S(1)} %broadcast_clamp_fusion), kind=kCustom, calls=%fused_computation.1 | custom fusion | bytes 8421376 | tf_op jit(solution)/shard_map/gather | solution.py:72
  453.5 5.4 %fusion.2 = f32[8192]{0:T(1024)} fusion(f32[8192,128]{1,0:T(8,128)} %gather_fusion.1, f32[32,256,128]{2,1,0:T(8,128)} %pad_maximum_fusion), kind=kLoop, calls=%fused_computation.16 | loop fusion | flops 2088960 | bytes 8421376 | tf_op jit(solution)/shard_map/reduce_sum | solution.py:72
  458.9 7.6 %all-to-all-start.5 = ((f32[32,1,256]{2,1,0:T(1,128)}), f32[32,1,256]{2,1,0:T(1,128)S(1)}, u32[]{:S(2)}, u32[]{:S(2)}) async-start(f32[32,1,256]{2,1,0:T(1,128)} %bitcast.21), calls=%async_computation.5 | async-start | bytes 65536 | tf_op jit(solution)/shard_map/all_to_all | solution.py:73
  466.5 3.4 fusion
  469.8 3.9 all-to-all-done.5
  (56 shorter events, 16.1 us)
Async XLA Ops:
  7.2 26.4 %copy-start = (f32[128,64]{0,1:T(8,128)S(1)}, f32[128,64]{0,1:T(8,128)}, u32[]{:S(2)}) copy-start(f32[128,64]{0,1:T(8,128)} %param.12) | copy-start | bytes 98308
  7.2 12.0 %copy-start.10 = (s32[1,1,32]{2,1,0:T(1,128)S(1)}, s32[1,1,32]{2,1,0:T(1,128)}, u32[]{:S(2)}) copy-start(s32[1,1,32]{2,1,0:T(1,128)} %param.10) | copy-start | bytes 388
  10.6 15.8 %all-to-all-start.2 = ((f32[32,1,256]{2,1,0:T(1,128)}), f32[32,1,256]{2,1,0:T(1,128)S(1)}, u32[]{:S(2)}, u32[]{:S(2)}) async-start(f32[32,1,256]{2,1,0:T(1,128)} %bitcast.6), calls=%async_computation.2 | async-start | bytes 65536 | tf_op jit(solution)/shard_map/all_to_all | solution.py:60
  26.5 8.1 %copy-start.6 = (f32[64,4096]{1,0:T(8,128)S(1)}, f32[64,4096]{1,0:T(8,128)}, u32[]{:S(2)}) copy-start(f32[64,4096]{1,0:T(8,128)} %param.13) | copy-start | bytes 3145732
  26.5 34.9 %all-to-all-start = ((f32[32,128,128]{2,1,0:T(8,128)}), f32[32,128,128]{2,1,0:T(8,128)S(1)}, u32[]{:S(2)}, u32[]{:S(2)}) async-start(f32[32,128,128]{2,1,0:T(8,128)} %get-tuple-element.12), calls=%async_computation | async-start | bytes 4194304 | tf_op jit(solution)/shard_map/all_to_all | solution.py:42
  33.6 68.2 %all-reduce.3.cloned.1.call-start = ((), (), s32[]{:S(2)}) async-start(), calls=%async_computation.8 | async-start | bytes 4325376 | tf_op jit(solution)/shard_map/psum | solution.py:45
  34.5 4.8 copy-start.8
  61.4 6.8 %copy-start.3 = (f32[32,128,128]{2,1,0:T(8,128)}, f32[32,128,128]{2,1,0:T(8,128)S(1)}, u32[]{:S(2)}) copy-start(f32[32,128,128]{2,1,0:T(8,128)S(1)} %all-to-all-done) | copy-start | bytes 6291460
  61.4 34.7 %all-to-all-start.1 = ((f32[32,128,128]{2,1,0:T(8,128)}), f32[32,128,128]{2,1,0:T(8,128)}, u32[]{:S(2)}, u32[]{:S(2)}) async-start(f32[32,128,128]{2,1,0:T(8,128)} %get-tuple-element.13), calls=%async_computation.1 | async-start | bytes 4194304 | tf_op jit(solution)/shard_map/all_to_all | solution.py:42
  68.1 145.2 %all-gather.5.cloned.1.call-start = ((), (), s32[]{:S(2)}) async-start(), calls=%async_computation.6 | async-start | bytes 10485760 | tf_op jit(solution)/shard_map/all_gather | solution.py:67
  128.9 1.3 copy-start.1
  213.3 5.4 %copy-start.7 = (f32[128,128]{1,0:T(8,128)S(1)}, f32[128,128]{1,0:T(8,128)}, u32[]{:S(2)}) copy-start(f32[128,128]{1,0:T(8,128)} %get-tuple-element.6) | copy-start | bytes 196612
  255.7 16.4 %copy-start.9 = (f32[2048]{0:T(1024)S(1)}, f32[2048]{0:T(1024)}, u32[]{:S(2)}) copy-start(f32[2048]{0:T(1024)} %param.7) | copy-start | bytes 24580
  255.7 15.0 %all-to-all-start.3 = ((f32[32,1,256]{2,1,0:T(1,128)}), f32[32,1,256]{2,1,0:T(1,128)S(1)}, u32[]{:S(2)}, u32[]{:S(2)}) async-start(f32[32,1,256]{2,1,0:T(1,128)} %bitcast.15), calls=%async_computation.3 | async-start | bytes 65536 | tf_op jit(solution)/shard_map/all_to_all | solution.py:73
  263.4 153.0 %all-gather.7.cloned.1.call-start = ((), (), s32[]{:S(2)}) async-start(), calls=%async_computation.7 | async-start | bytes 10485760 | tf_op jit(solution)/shard_map/all_gather | solution.py:67
  270.7 13.6 %copy-start.4 = (f32[32,128,128]{2,1,0:T(8,128)S(1)}, f32[32,128,128]{2,1,0:T(8,128)}, u32[]{:S(2)}) copy-start(f32[32,128,128]{2,1,0:T(8,128)} %copy-done.3) | copy-start | bytes 6291460
  334.6 1.3 copy-start.2
  453.5 12.9 %copy-start.5 = (f32[4096,128]{1,0:T(8,128)S(1)}, f32[4096,128]{1,0:T(8,128)}, u32[]{:S(2)}) copy-start(f32[4096,128]{1,0:T(8,128)} %reduce_sum.68) | copy-start | bytes 6291460
  458.9 14.8 %all-to-all-start.5 = ((f32[32,1,256]{2,1,0:T(1,128)}), f32[32,1,256]{2,1,0:T(1,128)S(1)}, u32[]{:S(2)}, u32[]{:S(2)}) async-start(f32[32,1,256]{2,1,0:T(1,128)} %bitcast.21), calls=%async_computation.5 | async-start | bytes 65536 | tf_op jit(solution)/shard_map/all_to_all | solution.py:73
Sparse Core Ops, SparseCore 0:
  39.5 62.2 all-reduce.2
  130.3 82.9 all-gather.4
  336.1 80.2 all-gather.6
